TPU v7x, 32 devices: a whole 2x2x4 slice. The times are simulated.
32 devices in a mesh: groups: 2 (over y), seq: 8 (over z, x), head: 2 (over core).
Axes of the slice: x: 2, y: 2, z: 4, core: 2. Of those that a mesh axis runs over, the one named last changes fastest.
Arguments:
- query_vectors: bfloat16 [2, 16384, 512], P(None, ('groups', 'seq'), 'head'), parts along dimension 1, may hold values from -8 to 8
- key_vectors: bfloat16 [2, 16384, 512], P(None, ('groups', 'seq'), 'head'), parts along dimension 1, may hold values from -8 to 8
- value_vectors: bfloat16 [2, 16384, 512], P(None, ('groups', 'seq'), 'head'), parts along dimension 1, may hold values from -12 to 12
Outputs:
- attended: bfloat16 [2, 16384, 512], P(None, ('groups', 'seq'), 'head'), parts along dimension 1
There are 2 independent parts, one for each index of `groups`. A program takes and returns all parts, laid end to end along the dimension named above; each array names one. Nothing has to cross between parts.
All inputs are finite; a program needn't handle non-finite values.
Results may differ from a plain program's by a relative error of at most 0.0039.
Values may be sent and summed in bfloat16 or wider, within the bound.
No kernel may reach another device: no remote copies, remote signals or barrier semaphores. Data moves between devices by JAX's collectives and lax.ppermute only.
A program may use at most 64 MiB of HBM per device.

v0:
```python
import math
import jax
import jax.numpy as jnp
from jax import lax
from jax.sharding import PartitionSpec as P

DH = 128
STRIDE = 1024


def shifted(block, axis, distance):
    devices = range(lax.axis_size(axis))
    route = [(i - distance, i) for i in devices if i - distance in devices]
    return lax.ppermute(block, axis, route)


def attend_columns(query_cols, key_cols, value_cols):
    score_scale = 1.0 / math.sqrt(DH)
    scores = (
        jnp.einsum("rchd,schd->chrs", query_cols, key_cols, preferred_element_type=jnp.float32)
        * score_scale
    )
    count = query_cols.shape[0]
    row_pos = jnp.arange(count, dtype=jnp.int32)[:, None]
    other_pos = jnp.arange(count, dtype=jnp.int32)[None, :]
    allowed = other_pos <= row_pos
    scores = jnp.where(allowed[None, None], scores, -jnp.inf)
    maxima = jnp.max(scores, axis=-1, keepdims=True)
    expo = jnp.exp(scores - maxima)
    weights = (expo / jnp.sum(expo, axis=-1, keepdims=True)).astype(jnp.bfloat16)
    return jnp.einsum(
        "chrs,schd->rchd", weights, value_cols, preferred_element_type=jnp.float32
    ).astype(jnp.bfloat16)


def local(query_vectors, key_vectors, value_vectors):
    local_tokens = query_vectors.shape[1]
    feature_width = query_vectors.shape[2]
    heads_here = feature_width // DH
    rows_here = local_tokens // STRIDE
    score_scale = 1.0 / math.sqrt(DH)
    prev_keys, prev_values = shifted(
        (key_vectors[0, local_tokens - STRIDE :], value_vectors[0, local_tokens - STRIDE :]),
        "seq",
        1,
    )
    ext_keys = jnp.concatenate([prev_keys, key_vectors[0]], axis=0).reshape(
        local_tokens + STRIDE, heads_here, DH
    )
    ext_values = jnp.concatenate([prev_values, value_vectors[0]], axis=0).reshape(
        local_tokens + STRIDE, heads_here, DH
    )
    queries = query_vectors[0].reshape(local_tokens, heads_here, DH)
    block_size = min(512, local_tokens)
    first_token = lax.axis_index("seq") * local_tokens

    def one_block(offset):
        query_block = lax.dynamic_slice_in_dim(queries, offset, block_size, 0)
        key_block = lax.dynamic_slice_in_dim(ext_keys, offset, STRIDE + block_size, 0)
        value_block = lax.dynamic_slice_in_dim(ext_values, offset, STRIDE + block_size, 0)
        scores = (
            jnp.einsum("qhd,khd->hqk", query_block, key_block, preferred_element_type=jnp.float32)
            * score_scale
        )
        query_pos = jnp.arange(block_size, dtype=jnp.int32)[:, None]
        key_pos = jnp.arange(STRIDE + block_size, dtype=jnp.int32)[None, :]
        allowed = (
            (key_pos > query_pos)
            & (key_pos <= STRIDE + query_pos)
            & (first_token + offset + key_pos >= STRIDE)
        )
        scores = jnp.where(allowed[None], scores, -jnp.inf)
        maxima = jnp.max(scores, axis=-1, keepdims=True)
        expo = jnp.exp(scores - maxima)
        weights = (expo / jnp.sum(expo, axis=-1, keepdims=True)).astype(jnp.bfloat16)
        return jnp.einsum(
            "hqk,khd->qhd", weights, value_block, preferred_element_type=jnp.float32
        ).astype(jnp.bfloat16)

    starts = jnp.arange(local_tokens // block_size, dtype=jnp.int32) * block_size
    row_out = lax.map(one_block, starts).reshape(local_tokens, feature_width)
    query_grid = query_vectors[1].reshape(rows_here, STRIDE, heads_here, DH)
    key_grid = key_vectors[1].reshape(rows_here, STRIDE, heads_here, DH)
    value_grid = value_vectors[1].reshape(rows_here, STRIDE, heads_here, DH)
    result = attend_columns(
        lax.all_to_all(query_grid, "seq", split_axis=1, concat_axis=0, tiled=True),
        lax.all_to_all(key_grid, "seq", split_axis=1, concat_axis=0, tiled=True),
        lax.all_to_all(value_grid, "seq", split_axis=1, concat_axis=0, tiled=True),
    )
    context = lax.all_to_all(result, "seq", split_axis=0, concat_axis=1, tiled=True)
    column_out = context.reshape(local_tokens, feature_width)
    return jnp.stack([row_out, column_out])


def solution(mesh):
    return jax.shard_map(
        local,
        mesh=mesh,
        in_specs=(
            P(None, ("groups", "seq"), "head"),
            P(None, ("groups", "seq"), "head"),
            P(None, ("groups", "seq"), "head"),
        ),
        out_specs=P(None, ("groups", "seq"), "head"),
        check_vma=False,
    )
```

profile of v0, /device:TPU:0, one launch (start us, length us, event | category | flops | bytes accessed | tf_op | source)
XLA Modules:
  0.0 122.1 jit_solution(14857121246988676300)
XLA Ops:
  0.0 1.3 %fusion.63 = (bf16[1,1024,256]{2,1,0:T(8,128)(2,1)S(1)}, bf16[1,1024,256]{2,1,0:T(8,128)(2,1)S(1)}) fusion(bf16[2,1024,256]{2,1,0:T(8,128)(2,1)} %param.5), kind=kLoop, calls=%fused_computation.57 | loop fusion | bytes 2097152 | tf_op jit(solution)/shard_map/slice | solution.py:53
  1.5 1.1 copy.71
  2.6 7.3 %all-to-all-start = ((bf16[1,1024,2,128]{3,2,0,1:T(2,128)(2,1)}), bf16[1,1024,2,128]{3,2,0,1:T(2,128)(2,1)S(1)}, u32[]{:S(2)}, u32[]{:S(2)}) async-start(bf16[1,1024,2,128]{3,2,0,1:T(2,128)(2,1)} %copy.71), calls=%async_computation | async-start | bytes 1048576 | tf_op jit(solution)/shard_map/all_to_all | solution.py:86
  9.9 0.9 fusion.62
  10.9 1.1 copy.74
  12.0 12.3 %all-to-all-done = bf16[1,1024,2,128]{3,2,0,1:T(2,128)(2,1)S(1)} async-done(((bf16[1,1024,2,128]{3,2,0,1:T(2,128)(2,1)}), bf16[1,1024,2,128]{3,2,0,1:T(2,128)(2,1)S(1)}, u32[]{:S(2)}, u32[]{:S(2)}) %all-to-all-start) | async-done | bytes 524320 | tf_op jit(solution)/shard_map/all_to_all | solution.py:86
  24.3 3.6 %all-to-all-start.1 = ((bf16[1,1024,2,128]{3,2,0,1:T(2,128)(2,1)}), bf16[1,1024,2,128]{3,2,0,1:T(2,128)(2,1)S(1)}, u32[]{:S(2)}, u32[]{:S(2)}) async-start(bf16[1,1024,2,128]{3,2,0,1:T(2,128)(2,1)} %copy.74), calls=%async_computation.1 | async-start | bytes 1048576 | tf_op jit(solution)/shard_map/all_to_all | solution.py:87
  28.0 2.1 %slice_bitcast_fusion = (bf16[1024,256]{1,0:T(8,128)(2,1)}, bf16[1,1024,256]{2,1,0:T(8,128)(2,1)S(1)}, bf16[1,1024,256]{2,1,0:T(8,128)(2,1)S(1)}) fusion(bf16[2,1024,256]{2,1,0:T(8,128)(2,1)} %param.7), kind=kLoop, calls=%fused_computation.54 | loop fusion | bytes 2621440 | tf_op jit(solution)/shard_map/squeeze | solution.py:43
  30.1 4.7 %collective-permute-start = (bf16[1024,256]{1,0:T(8,128)(2,1)}, bf16[1024,256]{1,0:T(8,128)(2,1)}, u32[]{:S(2)}, u32[]{:S(2)}) collective-permute-start(bf16[1024,256]{1,0:T(8,128)(2,1)} %get-tuple-element.89), channel_id=1, source_target_pairs={{0,2},{2,4},{4,6},{6,8},{8,10},{10,12},{12,14},{1,3},{3,5},{5,7},{... | collective-permute-start | bytes 1572872 | tf_op jit(solution)/shard_map/ppermute | solution.py:14
  34.8 1.2 %copy.97 = bf16[1,1024,256]{1,2,0:T(8,128)(2,1)S(1)} copy(bf16[1,1024,256]{2,1,0:T(8,128)(2,1)} %get-tuple-element.85) | data formatting | bytes 1048576
  36.0 3.4 %collective-permute-start.1 = (bf16[1024,256]{0,1:T(8,128)(2,1)S(1)}, bf16[1024,256]{0,1:T(8,128)(2,1)}, u32[]{:S(2)}, u32[]{:S(2)}) collective-permute-start(bf16[1024,256]{0,1:T(8,128)(2,1)S(1)} %bitcast.36), channel_id=1, source_target_pairs={{0,2},{2,4},{4,6},{6,8},{8,10},{10,12},{12,14},{1,3},{3,5},{5,7},{... | collective-permute-start | bytes 1572872 | tf_op jit(solution)/shard_map/ppermute | solution.py:14
  39.4 1.0 copy.96
  40.7 1.1 copy.80
  42.0 5.5 %collective-permute-done = bf16[1024,256]{1,0:T(8,128)(2,1)} collective-permute-done((bf16[1024,256]{1,0:T(8,128)(2,1)}, bf16[1024,256]{1,0:T(8,128)(2,1)}, u32[]{:S(2)}, u32[]{:S(2)}) %collective-permute-start) | collective-permute-done | bytes 524320 | tf_op jit(solution)/shard_map/ppermute | solution.py:14
  47.5 1.2 %copy.63 = bf16[1024,256]{0,1:T(8,128)(2,1)S(1)} copy(bf16[1024,256]{1,0:T(8,128)(2,1)} %collective-permute-done) | data formatting | bytes 1048576 | tf_op jit(solution)/shard_map/ppermute | solution.py:14
  48.7 9.1 %collective-permute-done.1 = bf16[1024,256]{0,1:T(8,128)(2,1)} collective-permute-done((bf16[1024,256]{0,1:T(8,128)(2,1)S(1)}, bf16[1024,256]{0,1:T(8,128)(2,1)}, u32[]{:S(2)}, u32[]{:S(2)}) %collective-permute-start.1) | collective-permute-done | bytes 524320 | tf_op jit(solution)/shard_map/ppermute | solution.py:14
  57.8 2.1 %pad_maximum_fusion.1 = bf16[2048,2,128]{0,2,1:T(8,128)(2,1)} fusion(bf16[1024,2,128]{0,2,1:T(8,128)(2,1)S(1)} %bitcast.37, bf16[1024,2,128]{0,2,1:T(8,128)(2,1)} %bitcast.8), kind=kLoop, calls=%fused_computation.38 | loop fusion | flops 2097152 | bytes 2097152 | tf_op jit(solution)/shard_map/concatenate | solution.py:47
  59.9 10.2 %all-to-all-start.2 = ((bf16[1,1024,2,128]{3,2,0,1:T(2,128)(2,1)}), bf16[1,1024,2,128]{3,2,0,1:T(2,128)(2,1)S(1)}, u32[]{:S(2)}, u32[]{:S(2)}) async-start(bf16[1,1024,2,128]{3,2,0,1:T(2,128)(2,1)} %copy.80), calls=%async_computation.2 | async-start | bytes 1048576 | tf_op jit(solution)/shard_map/all_to_all | solution.py:88
  70.1 1.1 pad_maximum_fusion
  71.2 0.7 fusion.48
  72.3 0.8 fusion.64
  73.6 11.2 %all-to-all-done.2 = bf16[1,1024,2,128]{3,2,0,1:T(2,128)(2,1)S(1)} async-done(((bf16[1,1024,2,128]{3,2,0,1:T(2,128)(2,1)}), bf16[1,1024,2,128]{3,2,0,1:T(2,128)(2,1)S(1)}, u32[]{:S(2)}, u32[]{:S(2)}) %all-to-all-start.2) | async-done | bytes 524320 | tf_op jit(solution)/shard_map/all_to_all | solution.py:88
  85.3 1.2 copy.84
  86.4 3.7 %all-to-all-start.3 = ((bf16[8,128,2,128]{3,2,1,0:T(2,128)(2,1)}), bf16[8,128,2,128]{3,2,1,0:T(2,128)(2,1)S(1)}, u32[]{:S(2)}, u32[]{:S(2)}) async-start(bf16[8,128,2,128]{3,2,1,0:T(2,128)(2,1)} %copy.84), calls=%async_computation.3 | async-start | bytes 1048576 | tf_op jit(solution)/shard_map/all_to_all | solution.py:90
  90.1 28.0 %while.10 = (s32[]{:T(128)}, bf16[2,512,2,128]{1,3,2,0:T(8,128)(2,1)}, s32[2]{0:T(128)S(1)}, bf16[2048,2,128]{0,2,1:T(8,128)(2,1)S(1)}, s32[]{:T(128)}, /*index=...) while((s32[]{:T(128)}, ...), condition=%wide.region_3.4_spmd, body=%wide.region_0.3_spmd.sunk | while | flops 1225399808 | bytes 5522644 | solution.py:81
  94.7 0.6 fusion.79
  95.3 3.6 %fusion.80 = f32[2,512]{1,0:T(2,128)S(1)} fusion(pred[512,1536]{1,0:T(8,128)(4,1)S(1)} %fusion.79, bf16[2048,2,128]{0,2,1:T(8,128)(2,1)S(1)} %get-tuple-element.165, s32[]{:T(128)S(6)} %select_n.38, bf16[1024,2,128]{0,2,1:T(8,128)(2,1)} %get-tuple-element.164, s32[]{:T(128)S(6)} %select_n.39), kind=kOutput, calls=%fused_computation.55.clone.1 | convolution fusion | flops 408946176 | bytes 1839112 | tf_op jit(solution)/shard_map/while/body/eval_jaxpr/sub | solution.py:74
  98.9 5.3 %fusion.81 = bf16[2,512,2,128]{1,3,2,0:T(8,128)(2,1)} fusion(bf16[2,512,2,128]{1,3,2,0:T(8,128)(2,1)} %get-tuple-element.149, s32[]{:T(128)S(6)} %copy.110, f32[2,512]{1,0:T(2,128)S(1)} %fusion.80, bf16[2048,2,128]{0,2,1:T(8,128)(2,1)S(1)} %get-tuple-element.162, s32[]{:T(128)S(6)} %select_n.38, pred[512,1536]{1,0:T(8,128)(4,1)S(1)} %fusion.79, ...), kind=kOutput, calls=%fused_computation.15.clone.1 | convolution fusion | flops 813304320 | bytes 2889728 | tf_op jit(solution)/shard_map/while/body/eval_jaxpr/hqk,khd->qhd/dot_general | solution.py:76
  109.3 3.6 %fusion.80 = f32[2,512]{1,0:T(2,128)S(1)} fusion(pred[512,1536]{1,0:T(8,128)(4,1)S(1)} %fusion.79, bf16[2048,2,128]{0,2,1:T(8,128)(2,1)S(1)} %get-tuple-element.165, s32[]{:T(128)S(6)} %select_n.38, bf16[1024,2,128]{0,2,1:T(8,128)(2,1)} %get-tuple-element.164, s32[]{:T(128)S(6)} %select_n.39), kind=kOutput, calls=%fused_computation.55.clone.1 | convolution fusion | flops 408946176 | bytes 1839112 | tf_op jit(solution)/shard_map/while/body/eval_jaxpr/sub | solution.py:74
  112.9 5.3 %fusion.81 = bf16[2,512,2,128]{1,3,2,0:T(8,128)(2,1)} fusion(bf16[2,512,2,128]{1,3,2,0:T(8,128)(2,1)} %get-tuple-element.149, s32[]{:T(128)S(6)} %copy.110, f32[2,512]{1,0:T(2,128)S(1)} %fusion.80, bf16[2048,2,128]{0,2,1:T(8,128)(2,1)S(1)} %get-tuple-element.162, s32[]{:T(128)S(6)} %select_n.38, pred[512,1536]{1,0:T(8,128)(4,1)S(1)} %fusion.79, ...), kind=kOutput, calls=%fused_computation.15.clone.1 | convolution fusion | flops 813304320 | bytes 2889728 | tf_op jit(solution)/shard_map/while/body/eval_jaxpr/hqk,khd->qhd/dot_general | solution.py:76
  118.2 1.6 %copy.69 = bf16[2,512,2,128]{1,0,3,2:T(2,128)(2,1)S(1)} copy(bf16[2,512,2,128]{1,3,2,0:T(8,128)(2,1)} %get-tuple-element.42) | data formatting | bytes 1048576 | tf_op jit(solution)/shard_map/while | solution.py:81
  120.8 1.3 %copy.86 = bf16[2,1024,256]{2,1,0:T(8,128)(2,1)} copy(bf16[2,1024,256]{1,2,0:T(8,128)(2,1)S(1)} %pad_maximum_fusion.2) | data formatting | bytes 2097152 | tf_op jit(solution)/shard_map/stack | solution.py:92
  (30 shorter events, 5.0 us)
Async XLA Ops:
  1.5 8.4 %copy-start = (bf16[2,1024,256]{2,1,0:T(8,128)(2,1)S(1)}, bf16[2,1024,256]{2,1,0:T(8,128)(2,1)}, u32[]{:S(2)}) copy-start(bf16[2,1024,256]{2,1,0:T(8,128)(2,1)} %param.6) | copy-start | bytes 3145732
  2.6 21.7 %all-to-all-start = ((bf16[1,1024,2,128]{3,2,0,1:T(2,128)(2,1)}), bf16[1,1024,2,128]{3,2,0,1:T(2,128)(2,1)S(1)}, u32[]{:S(2)}, u32[]{:S(2)}) async-start(bf16[1,1024,2,128]{3,2,0,1:T(2,128)(2,1)} %copy.71), calls=%async_computation | async-start | bytes 1048576 | tf_op jit(solution)/shard_map/all_to_all | solution.py:86
  24.3 35.5 %all-to-all-start.1 = ((bf16[1,1024,2,128]{3,2,0,1:T(2,128)(2,1)}), bf16[1,1024,2,128]{3,2,0,1:T(2,128)(2,1)S(1)}, u32[]{:S(2)}, u32[]{:S(2)}) async-start(bf16[1,1024,2,128]{3,2,0,1:T(2,128)(2,1)} %copy.74), calls=%async_computation.1 | async-start | bytes 1048576 | tf_op jit(solution)/shard_map/all_to_all | solution.py:87
  30.1 17.4 %collective-permute-start = (bf16[1024,256]{1,0:T(8,128)(2,1)}, bf16[1024,256]{1,0:T(8,128)(2,1)}, u32[]{:S(2)}, u32[]{:S(2)}) collective-permute-start(bf16[1024,256]{1,0:T(8,128)(2,1)} %get-tuple-element.89), channel_id=1, source_target_pairs={{0,2},{2,4},{4,6},{6,8},{8,10},{10,12},{12,14},{1,3},{3,5},{5,7},{... | collective-permute-start | bytes 1572872 | tf_op jit(solution)/shard_map/ppermute | solution.py:14
  36.0 21.7 %collective-permute-start.1 = (bf16[1024,256]{0,1:T(8,128)(2,1)S(1)}, bf16[1024,256]{0,1:T(8,128)(2,1)}, u32[]{:S(2)}, u32[]{:S(2)}) collective-permute-start(bf16[1024,256]{0,1:T(8,128)(2,1)S(1)} %bitcast.36), channel_id=1, source_target_pairs={{0,2},{2,4},{4,6},{6,8},{8,10},{10,12},{12,14},{1,3},{3,5},{5,7},{... | collective-permute-start | bytes 1572872 | tf_op jit(solution)/shard_map/ppermute | solution.py:14
  59.9 24.9 %all-to-all-start.2 = ((bf16[1,1024,2,128]{3,2,0,1:T(2,128)(2,1)}), bf16[1,1024,2,128]{3,2,0,1:T(2,128)(2,1)S(1)}, u32[]{:S(2)}, u32[]{:S(2)}) async-start(bf16[1,1024,2,128]{3,2,0,1:T(2,128)(2,1)} %copy.80), calls=%async_computation.2 | async-start | bytes 1048576 | tf_op jit(solution)/shard_map/all_to_all | solution.py:88
  85.2 4.9 %copy-start.1 = (bf16[2048,2,128]{0,2,1:T(8,128)(2,1)S(1)}, bf16[2048,2,128]{0,2,1:T(8,128)(2,1)}, u32[]{:S(2)}) copy-start(bf16[2048,2,128]{0,2,1:T(8,128)(2,1)} %pad_maximum_fusion.1) | copy-start | bytes 3145732
  85.2 4.9 %copy-start.2 = (bf16[2048,2,128]{0,2,1:T(8,128)(2,1)S(1)}, bf16[2048,2,128]{0,2,1:T(8,128)(2,1)}, u32[]{:S(2)}) copy-start(bf16[2048,2,128]{0,2,1:T(8,128)(2,1)} %pad_maximum_fusion) | copy-start | bytes 3145732
  86.4 33.7 %all-to-all-start.3 = ((bf16[8,128,2,128]{3,2,1,0:T(2,128)(2,1)}), bf16[8,128,2,128]{3,2,1,0:T(2,128)(2,1)S(1)}, u32[]{:S(2)}, u32[]{:S(2)}) async-start(bf16[8,128,2,128]{3,2,1,0:T(2,128)(2,1)} %copy.84), calls=%async_computation.3 | async-start | bytes 1048576 | tf_op jit(solution)/shard_map/all_to_all | solution.py:90
where the time goes:
time: 123 us; the launch traced here: 122 us
  waiting for transfers between devices  38 us (31%)
  starting transfers between devices  32.9 us (27%)
  local copies, waits for them, and re-layouts  18.9 us (15%)
  matrix products  18.9 us (15%)
  loops' own time  7.82 us (6%)
  other arithmetic  5.39 us (4%)
    ppermute x2, waiting for transfers between devices, shifted(): return lax.ppermute(block, axis, route)  14.5 us
    all_to_all x1, waiting for transfers between devices, local(): lax.all_to_all(query_grid, 'seq', split_axis=1, concat_axis=0, tiled=True)  12.3 us
    all_to_all x1, waiting for transfers between devices, local(): lax.all_to_all(value_grid, 'seq', split_axis=1, concat_axis=0, tiled=True)  11.2 us
    dot_general x2, matrix products, one_block(): jnp.einsum('hqk,khd->qhd', weights, value_block, preferred_element_type=j...  10.6 us
    all_to_all x1, starting transfers between devices, local(): lax.all_to_all(value_grid, 'seq', split_axis=1, concat_axis=0, tiled=True)  10.2 us
    ppermute x2, starting transfers between devices, shifted(): return lax.ppermute(block, axis, route)  8.12 us
    another operation x1, loops' own time, local(): row_out = lax.map(one_block, starts).reshape(local_tokens, feature_width)  7.82 us
    all_to_all x1, starting transfers between devices, local(): lax.all_to_all(query_grid, 'seq', split_axis=1, concat_axis=0, tiled=True)  7.25 us
  transfers between devices with their start and end apart: 6, of which 4 were waited for; matrix products, arithmetic and copies ran while one was open for 30% of the time, Pallas kernels for 0%

commit v1 on v0

--- a/solution.py
+++ b/solution.py
@@ -6,6 +6,28 @@
 
 DH = 128
 STRIDE = 1024
+
+
+def cut_along(x, dim, peers):
+    before, after = (x.shape[:dim], x.shape[dim + 1 :])
+    return jnp.moveaxis(x.reshape(*before, peers, -1, *after), dim, 0)
+
+
+def joined_along(tiles, dim):
+    dims = list(tiles.shape[1:])
+    dims[dim] *= tiles.shape[0]
+    return jnp.moveaxis(tiles, 0, dim).reshape(dims)
+
+
+def exchange_in_pairs(shard, axis, split_dim, concat_dim):
+    size, here = (lax.axis_size(axis), lax.axis_index(axis))
+    blocks = cut_along(shard, split_dim, size)
+    done = [blocks[here]]
+    for step in range(1, size):
+        sent = blocks[here ^ step]
+        done.append(lax.ppermute(sent, axis, [(i, i ^ step) for i in range(size)]))
+    blocks = jnp.stack(done)[here ^ jnp.arange(size)]
+    return joined_along(blocks, concat_dim)
 
 
 def shifted(block, axis, distance):
@@ -83,7 +105,7 @@
     key_grid = key_vectors[1].reshape(rows_here, STRIDE, heads_here, DH)
     value_grid = value_vectors[1].reshape(rows_here, STRIDE, heads_here, DH)
     result = attend_columns(
-        lax.all_to_all(query_grid, "seq", split_axis=1, concat_axis=0, tiled=True),
+        exchange_in_pairs(query_grid, "seq", 1, 0),
         lax.all_to_all(key_grid, "seq", split_axis=1, concat_axis=0, tiled=True),
         lax.all_to_all(value_grid, "seq", split_axis=1, concat_axis=0, tiled=True),
     )

time: 123 us -> 110 us (0.89)
  waiting for transfers between devices: 38 us -> 14.8 us
  starting transfers between devices: 32.9 us -> 39.2 us
  local copies, waits for them, and re-layouts: 18.9 us -> 22.8 us
    ppermute x0 -> x7, starting transfers between devices: none -> 14.2 us  [exchange_in_pairs(): done.append(lax.ppermute(sent, axis, [(i, i ^ step) for i in range(size)]))]
    all_to_all x1 -> x0, waiting for transfers between devices: 12.3 us -> none  [local(): lax.all_to_all(query_grid, 'seq', split_axis=1, concat_axis=0, tiled=True)]
    all_to_all x1 -> x0, starting transfers between devices: 7.25 us -> none  [local(): lax.all_to_all(query_grid, 'seq', split_axis=1, concat_axis=0, tiled=True)]
    ppermute x2, waiting for transfers between devices: 14.5 us -> 8.52 us  [shifted(): return lax.ppermute(block, axis, route)]
    all_to_all x1, waiting for transfers between devices: 11.2 us -> 6.27 us  [local(): lax.all_to_all(value_grid, 'seq', split_axis=1, concat_axis=0, tiled=True)]
    all_to_all x1, starting transfers between devices: 3.67 us -> 7.01 us  [local(): lax.all_to_all(result, 'seq', split_axis=0, concat_axis=1, tiled=True)]
    dynamic_slice x0 -> x8, local copies, waits for them, and re-layouts: none -> 2.97 us  [exchange_in_pairs(): sent = blocks[here ^ step]]
    all_to_all x1, starting transfers between devices: 10.2 us -> 7.39 us  [local(): lax.all_to_all(value_grid, 'seq', split_axis=1, concat_axis=0, tiled=True)]
  transfers between devices with their start and end apart: 6 -> 12, of which waited for: 4 -> 3; matrix products, arithmetic and copies ran while one was open for 30% -> 38% of each run, Pallas kernels for 0% -> 0%
where the time goes in v1:
time: 110 us; the launch traced here: 109 us
  starting transfers between devices  39.2 us (36%)
  local copies, waits for them, and re-layouts  22.8 us (21%)
  matrix products  18.9 us (17%)
  waiting for transfers between devices  14.8 us (13%)
  loops' own time  7.82 us (7%)
  other arithmetic  5.41 us (5%)
    ppermute x7, starting transfers between devices, exchange_in_pairs(): done.append(lax.ppermute(sent, axis, [(i, i ^ step) for i in range(size)]))  14.2 us
    dot_general x2, matrix products, one_block(): jnp.einsum('hqk,khd->qhd', weights, value_block, preferred_element_type=j...  10.6 us
    ppermute x2, waiting for transfers between devices, shifted(): return lax.ppermute(block, axis, route)  8.52 us
    another operation x1, loops' own time, local(): row_out = lax.map(one_block, starts).reshape(local_tokens, feature_width)  7.82 us
    all_to_all x1, starting transfers between devices, local(): lax.all_to_all(value_grid, 'seq', split_axis=1, concat_axis=0, tiled=True)  7.39 us
    sub x2, matrix products, one_block(): expo = jnp.exp(scores - maxima)  7.12 us
    all_to_all x1, starting transfers between devices, local(): lax.all_to_all(result, 'seq', split_axis=0, concat_axis=1, tiled=True)  7.01 us
    all_to_all x1, waiting for transfers between devices, local(): lax.all_to_all(value_grid, 'seq', split_axis=1, concat_axis=0, tiled=True)  6.27 us
  transfers between devices with their start and end apart: 12, of which 3 were waited for; matrix products, arithmetic and copies ran while one was open for 38% of the time, Pallas kernels for 0%

profile of v1, /device:TPU:0, one launch (start us, length us, event | category | flops | bytes accessed | tf_op | source)
XLA Modules:
  0.0 109.3 jit_solution(15931970521250855006)
XLA Ops:
  0.0 1.3 %fusion.64 = (bf16[1,1024,256]{2,1,0:T(8,128)(2,1)S(1)}, bf16[1,1024,256]{2,1,0:T(8,128)(2,1)S(1)}) fusion(bf16[2,1024,256]{2,1,0:T(8,128)(2,1)} %param.5), kind=kLoop, calls=%fused_computation.84 | loop fusion | bytes 2097152 | tf_op jit(solution)/shard_map/slice | solution.py:75
  2.5 2.9 %collective-permute-start.2 = (bf16[1,128,2,128]{3,1,2,0:T(8,128)(2,1)}, bf16[1,128,2,128]{3,1,2,0:T(8,128)(2,1)}, u32[]{:S(2)}, u32[]{:S(2)}) collective-permute-start(bf16[1,128,2,128]{3,1,2,0:T(8,128)(2,1)} %bitcast.61), channel_id=1, source_target_pairs={{0,2},{2,0},{4,6},{6,4},{8,10},{10,8},{12,14},{14,12},{1,3},{3,1},... | collective-permute-start | bytes 196616 | tf_op jit(solution)/shard_map/ppermute | solution.py:28
  6.1 1.6 %collective-permute-start.3 = (bf16[1,128,2,128]{3,1,2,0:T(8,128)(2,1)}, bf16[1,128,2,128]{3,1,2,0:T(8,128)(2,1)}, u32[]{:S(2)}, u32[]{:S(2)}) collective-permute-start(bf16[1,128,2,128]{3,1,2,0:T(8,128)(2,1)} %bitcast.60), channel_id=1, source_target_pairs={{0,4},{2,6},{4,0},{6,2},{8,12},{10,14},{12,8},{14,10},{1,5},{3,7},... | collective-permute-start | bytes 196616 | tf_op jit(solution)/shard_map/ppermute | solution.py:28
  8.9 3.0 %collective-permute-start.5 = (bf16[1,128,2,128]{3,1,2,0:T(8,128)(2,1)}, bf16[1,128,2,128]{3,1,2,0:T(8,128)(2,1)S(1)}, u32[]{:S(2)}, u32[]{:S(2)}) collective-permute-start(bf16[1,128,2,128]{3,1,2,0:T(8,128)(2,1)} %bitcast.58), channel_id=1, source_target_pairs={{0,8},{2,10},{4,12},{6,14},{8,0},{10,2},{12,4},{14,6},{1,9},{3,11}... | collective-permute-start | bytes 196616 | tf_op jit(solution)/shard_map/ppermute | solution.py:28
  11.9 1.3 %collective-permute-start.6 = (bf16[1,128,2,128]{3,1,2,0:T(8,128)(2,1)S(1)}, bf16[1,128,2,128]{3,1,2,0:T(8,128)(2,1)S(1)}, u32[]{:S(2)}, u32[]{:S(2)}) collective-permute-start(bf16[1,128,2,128]{3,1,2,0:T(8,128)(2,1)S(1)} %bitcast.76), channel_id=1, source_target_pairs={{0,10},{2,8},{4,14},{6,12},{8,2},{10,0},{12,6},{14,4},{1,11},{3,9}... | collective-permute-start | bytes 196616 | tf_op jit(solution)/shard_map/ppermute | solution.py:28
  13.6 1.1 %copy.93 = bf16[1,1024,2,128]{3,2,0,1:T(2,128)(2,1)} copy(bf16[1,1024,2,128]{1,3,2,0:T(8,128)(2,1)S(1)} %bitcast.67) | data formatting | bytes 1048576 | tf_op jit(solution)/shard_map/reshape;squeeze | solution.py:105
  14.7 4.9 %all-to-all-start = ((bf16[1,1024,2,128]{3,2,0,1:T(2,128)(2,1)}), bf16[1,1024,2,128]{3,2,0,1:T(2,128)(2,1)S(1)}, u32[]{:S(2)}, u32[]{:S(2)}) async-start(bf16[1,1024,2,128]{3,2,0,1:T(2,128)(2,1)} %copy.93), calls=%async_computation | async-start | bytes 1048576 | tf_op jit(solution)/shard_map/all_to_all | solution.py:109
  20.3 2.1 %slice_bitcast_fusion = (bf16[1024,256]{1,0:T(8,128)(2,1)}, bf16[1,1024,256]{2,1,0:T(8,128)(2,1)S(1)}, bf16[1,1024,256]{2,1,0:T(8,128)(2,1)S(1)}) fusion(bf16[2,1024,256]{2,1,0:T(8,128)(2,1)} %param.7), kind=kLoop, calls=%fused_computation.81 | loop fusion | bytes 2621440 | tf_op jit(solution)/shard_map/squeeze | solution.py:65
  22.6 1.1 %copy.99 = bf16[1,1024,2,128]{3,2,0,1:T(2,128)(2,1)} copy(bf16[1,1024,2,128]{1,3,2,0:T(8,128)(2,1)S(1)} %bitcast.68) | data formatting | bytes 1048576 | tf_op jit(solution)/shard_map/reshape;squeeze | solution.py:106
  24.1 1.0 copy.115
  25.2 3.8 %collective-permute-start.7 = (bf16[1,128,2,128]{3,1,2,0:T(8,128)(2,1)S(1)}, bf16[1,128,2,128]{3,1,2,0:T(8,128)(2,1)S(1)}, u32[]{:S(2)}, u32[]{:S(2)}) collective-permute-start(bf16[1,128,2,128]{3,1,2,0:T(8,128)(2,1)S(1)} %bitcast.78), channel_id=1, source_target_pairs={{0,12},{2,14},{4,8},{6,10},{8,4},{10,6},{12,0},{14,2},{1,13},{3,15... | collective-permute-start | bytes 196616 | tf_op jit(solution)/shard_map/ppermute | solution.py:28
  29.0 0.9 bitcast_dynamic-update-slice_fusion.6
  29.8 1.5 %collective-permute-start.8 = (bf16[1,128,2,128]{3,1,2,0:T(8,128)(2,1)S(1)}, bf16[1,128,2,128]{3,1,2,0:T(8,128)(2,1)S(1)}, u32[]{:S(2)}, u32[]{:S(2)}) collective-permute-start(bf16[1,128,2,128]{3,1,2,0:T(8,128)(2,1)S(1)} %bitcast.77), channel_id=1, source_target_pairs={{0,14},{2,12},{4,10},{6,8},{8,6},{10,4},{12,2},{14,0},{1,15},{3,13... | collective-permute-start | bytes 196616 | tf_op jit(solution)/shard_map/ppermute | solution.py:28
  31.4 0.9 bitcast_dynamic-update-slice_fusion.5
  32.2 2.7 %collective-permute-start = (bf16[1024,256]{1,0:T(8,128)(2,1)}, bf16[1024,256]{1,0:T(8,128)(2,1)}, u32[]{:S(2)}, u32[]{:S(2)}) collective-permute-start(bf16[1024,256]{1,0:T(8,128)(2,1)} %get-tuple-element.89), channel_id=1, source_target_pairs={{0,2},{2,4},{4,6},{6,8},{8,10},{10,12},{12,14},{1,3},{3,5},{5,7},{... | collective-permute-start | bytes 1572872 | tf_op jit(solution)/shard_map/ppermute | solution.py:36
  35.0 0.9 bitcast_dynamic-update-slice_fusion.4
  35.8 3.1 %collective-permute-start.1 = (bf16[1024,256]{0,1:T(8,128)(2,1)S(1)}, bf16[1024,256]{0,1:T(8,128)(2,1)}, u32[]{:S(2)}, u32[]{:S(2)}) collective-permute-start(bf16[1024,256]{0,1:T(8,128)(2,1)S(1)} %bitcast.70), channel_id=1, source_target_pairs={{0,2},{2,4},{4,6},{6,8},{8,10},{10,12},{12,14},{1,3},{3,5},{5,7},{... | collective-permute-start | bytes 1572872 | tf_op jit(solution)/shard_map/ppermute | solution.py:36
  39.6 7.7 %collective-permute-done = bf16[1024,256]{1,0:T(8,128)(2,1)} collective-permute-done((bf16[1024,256]{1,0:T(8,128)(2,1)}, bf16[1024,256]{1,0:T(8,128)(2,1)}, u32[]{:S(2)}, u32[]{:S(2)}) %collective-permute-start) | collective-permute-done | bytes 524320 | tf_op jit(solution)/shard_map/ppermute | solution.py:36
  47.4 1.2 %copy.76 = bf16[1024,256]{0,1:T(8,128)(2,1)S(1)} copy(bf16[1024,256]{1,0:T(8,128)(2,1)} %collective-permute-done) | data formatting | bytes 1048576 | tf_op jit(solution)/shard_map/ppermute | solution.py:36
  48.6 1.1 pad_maximum_fusion
  49.7 7.4 %all-to-all-start.1 = ((bf16[1,1024,2,128]{3,2,0,1:T(2,128)(2,1)}), bf16[1,1024,2,128]{3,2,0,1:T(2,128)(2,1)S(1)}, u32[]{:S(2)}, u32[]{:S(2)}) async-start(bf16[1,1024,2,128]{3,2,0,1:T(2,128)(2,1)} %copy.99), calls=%async_computation.1 | async-start | bytes 1048576 | tf_op jit(solution)/shard_map/all_to_all | solution.py:110
  57.9 2.1 %pad_maximum_fusion.1 = bf16[2048,2,128]{0,2,1:T(8,128)(2,1)} fusion(bf16[1024,2,128]{0,2,1:T(8,128)(2,1)S(1)} %bitcast.71, bf16[1024,2,128]{0,2,1:T(8,128)(2,1)} %bitcast.8), kind=kLoop, calls=%fused_computation.39 | loop fusion | flops 2097152 | bytes 2097152 | tf_op jit(solution)/shard_map/concatenate | solution.py:69
  62.4 6.3 %all-to-all-done.1 = bf16[1,1024,2,128]{3,2,0,1:T(2,128)(2,1)S(1)} async-done(((bf16[1,1024,2,128]{3,2,0,1:T(2,128)(2,1)}), bf16[1,1024,2,128]{3,2,0,1:T(2,128)(2,1)S(1)}, u32[]{:S(2)}, u32[]{:S(2)}) %all-to-all-start.1) | async-done | bytes 524320 | tf_op jit(solution)/shard_map/all_to_all | solution.py:110
  69.1 1.2 %copy.103 = bf16[8,128,2,128]{3,2,1,0:T(2,128)(2,1)} copy(bf16[8,128,2,128]{3,0,2,1:T(8,128)(2,1)S(1)} %fusion.44) | data formatting | bytes 1048576 | tf_op jit(solution)/shard_map/convert_element_type | solution.py:55
  70.3 7.0 %all-to-all-start.2 = ((bf16[8,128,2,128]{3,2,1,0:T(2,128)(2,1)}), bf16[8,128,2,128]{3,2,1,0:T(2,128)(2,1)S(1)}, u32[]{:S(2)}, u32[]{:S(2)}) async-start(bf16[8,128,2,128]{3,2,1,0:T(2,128)(2,1)} %copy.103), calls=%async_computation.2 | async-start | bytes 1048576 | tf_op jit(solution)/shard_map/all_to_all | solution.py:112
  77.4 28.0 %while.10 = (s32[]{:T(128)}, bf16[2,512,2,128]{1,3,2,0:T(8,128)(2,1)}, s32[2]{0:T(128)S(1)}, bf16[2048,2,128]{0,2,1:T(8,128)(2,1)S(1)}, s32[]{:T(128)}, /*index=...) while((s32[]{:T(128)}, ...), condition=%wide.region_3.4_spmd, body=%wide.region_0.3_spmd.sunk | while | flops 1225399808 | bytes 5522636 | solution.py:103
  82.5 3.6 %fusion.81 = f32[2,512]{1,0:T(2,128)S(1)} fusion(pred[512,1536]{1,0:T(8,128)(4,1)S(1)} %fusion.80, bf16[2048,2,128]{0,2,1:T(8,128)(2,1)S(1)} %get-tuple-element.173, s32[]{:T(128)S(6)} %select_n.84, bf16[1024,2,128]{0,2,1:T(8,128)(2,1)} %get-tuple-element.172, s32[]{:T(128)S(6)} %select_n.85), kind=kOutput, calls=%fused_computation.82.clone.1 | convolution fusion | flops 408946176 | bytes 1839112 | tf_op jit(solution)/shard_map/while/body/eval_jaxpr/sub | solution.py:96
  86.1 5.3 %fusion.82 = bf16[2,512,2,128]{1,3,2,0:T(8,128)(2,1)} fusion(bf16[2,512,2,128]{1,3,2,0:T(8,128)(2,1)} %get-tuple-element.157, s32[]{:T(128)} %get-tuple-element.156, f32[2,512]{1,0:T(2,128)S(1)} %fusion.81, bf16[2048,2,128]{0,2,1:T(8,128)(2,1)S(1)} %get-tuple-element.170, s32[]{:T(128)S(6)} %select_n.84, pred[512,1536]{1,0:T(8,128)(4,1)S(1)} %fusion.80, ...), kind=kOutput, calls=%fused_computation.16.clone.1 | convolution fusion | flops 813304320 | bytes 2889728 | tf_op jit(solution)/shard_map/while/body/eval_jaxpr/hqk,khd->qhd/dot_general | solution.py:98
  96.5 3.6 %fusion.81 = f32[2,512]{1,0:T(2,128)S(1)} fusion(pred[512,1536]{1,0:T(8,128)(4,1)S(1)} %fusion.80, bf16[2048,2,128]{0,2,1:T(8,128)(2,1)S(1)} %get-tuple-element.173, s32[]{:T(128)S(6)} %select_n.84, bf16[1024,2,128]{0,2,1:T(8,128)(2,1)} %get-tuple-element.172, s32[]{:T(128)S(6)} %select_n.85), kind=kOutput, calls=%fused_computation.82.clone.1 | convolution fusion | flops 408946176 | bytes 1839112 | tf_op jit(solution)/shard_map/while/body/eval_jaxpr/sub | solution.py:96
  100.0 5.3 %fusion.82 = bf16[2,512,2,128]{1,3,2,0:T(8,128)(2,1)} fusion(bf16[2,512,2,128]{1,3,2,0:T(8,128)(2,1)} %get-tuple-element.157, s32[]{:T(128)} %get-tuple-element.156, f32[2,512]{1,0:T(2,128)S(1)} %fusion.81, bf16[2048,2,128]{0,2,1:T(8,128)(2,1)S(1)} %get-tuple-element.170, s32[]{:T(128)S(6)} %select_n.84, pred[512,1536]{1,0:T(8,128)(4,1)S(1)} %fusion.80, ...), kind=kOutput, calls=%fused_computation.16.clone.1 | convolution fusion | flops 813304320 | bytes 2889728 | tf_op jit(solution)/shard_map/while/body/eval_jaxpr/hqk,khd->qhd/dot_general | solution.py:98
  105.4 1.6 %copy.82 = bf16[2,512,2,128]{1,0,3,2:T(2,128)(2,1)S(1)} copy(bf16[2,512,2,128]{1,3,2,0:T(8,128)(2,1)} %get-tuple-element.42) | data formatting | bytes 1048576 | tf_op jit(solution)/shard_map/while | solution.py:103
  108.0 1.3 %copy.105 = bf16[2,1024,256]{2,1,0:T(8,128)(2,1)} copy(bf16[2,1024,256]{1,2,0:T(8,128)(2,1)S(1)} %pad_maximum_fusion.2) | data formatting | bytes 2097152 | tf_op jit(solution)/shard_map/stack | solution.py:114
  (62 shorter events, 12.5 us)
Async XLA Ops:
  1.4 11.9 %copy-start = (bf16[2,1024,256]{2,1,0:T(8,128)(2,1)S(1)}, bf16[2,1024,256]{2,1,0:T(8,128)(2,1)}, u32[]{:S(2)}) copy-start(bf16[2,1024,256]{2,1,0:T(8,128)(2,1)} %param.6) | copy-start | bytes 3145732
  2.5 22.7 %collective-permute-start.2 = (bf16[1,128,2,128]{3,1,2,0:T(8,128)(2,1)}, bf16[1,128,2,128]{3,1,2,0:T(8,128)(2,1)}, u32[]{:S(2)}, u32[]{:S(2)}) collective-permute-start(bf16[1,128,2,128]{3,1,2,0:T(8,128)(2,1)} %bitcast.61), channel_id=1, source_target_pairs={{0,2},{2,0},{4,6},{6,4},{8,10},{10,8},{12,14},{14,12},{1,3},{3,1},... | collective-permute-start | bytes 196616 | tf_op jit(solution)/shard_map/ppermute | solution.py:28
  6.1 23.8 %collective-permute-start.3 = (bf16[1,128,2,128]{3,1,2,0:T(8,128)(2,1)}, bf16[1,128,2,128]{3,1,2,0:T(8,128)(2,1)}, u32[]{:S(2)}, u32[]{:S(2)}) collective-permute-start(bf16[1,128,2,128]{3,1,2,0:T(8,128)(2,1)} %bitcast.60), channel_id=1, source_target_pairs={{0,4},{2,6},{4,0},{6,2},{8,12},{10,14},{12,8},{14,10},{1,5},{3,7},... | collective-permute-start | bytes 196616 | tf_op jit(solution)/shard_map/ppermute | solution.py:28
  8.3 23.9 %collective-permute-start.4 = (bf16[1,128,2,128]{3,1,2,0:T(8,128)(2,1)}, bf16[1,128,2,128]{3,1,2,0:T(8,128)(2,1)}, u32[]{:S(2)}, u32[]{:S(2)}) collective-permute-start(bf16[1,128,2,128]{3,1,2,0:T(8,128)(2,1)} %bitcast.59), channel_id=1, source_target_pairs={{0,6},{2,4},{4,2},{6,0},{8,14},{10,12},{12,10},{14,8},{1,7},{3,5},... | collective-permute-start | bytes 196616 | tf_op jit(solution)/shard_map/ppermute | solution.py:28
  8.9 26.9 %collective-permute-start.5 = (bf16[1,128,2,128]{3,1,2,0:T(8,128)(2,1)}, bf16[1,128,2,128]{3,1,2,0:T(8,128)(2,1)S(1)}, u32[]{:S(2)}, u32[]{:S(2)}) collective-permute-start(bf16[1,128,2,128]{3,1,2,0:T(8,128)(2,1)} %bitcast.58), channel_id=1, source_target_pairs={{0,8},{2,10},{4,12},{6,14},{8,0},{10,2},{12,4},{14,6},{1,9},{3,11}... | collective-permute-start | bytes 196616 | tf_op jit(solution)/shard_map/ppermute | solution.py:28
  11.9 27.0 %collective-permute-start.6 = (bf16[1,128,2,128]{3,1,2,0:T(8,128)(2,1)S(1)}, bf16[1,128,2,128]{3,1,2,0:T(8,128)(2,1)S(1)}, u32[]{:S(2)}, u32[]{:S(2)}) collective-permute-start(bf16[1,128,2,128]{3,1,2,0:T(8,128)(2,1)S(1)} %bitcast.76), channel_id=1, source_target_pairs={{0,10},{2,8},{4,14},{6,12},{8,2},{10,0},{12,6},{14,4},{1,11},{3,9}... | collective-permute-start | bytes 196616 | tf_op jit(solution)/shard_map/ppermute | solution.py:28
  14.7 35.0 %all-to-all-start = ((bf16[1,1024,2,128]{3,2,0,1:T(2,128)(2,1)}), bf16[1,1024,2,128]{3,2,0,1:T(2,128)(2,1)S(1)}, u32[]{:S(2)}, u32[]{:S(2)}) async-start(bf16[1,1024,2,128]{3,2,0,1:T(2,128)(2,1)} %copy.93), calls=%async_computation | async-start | bytes 1048576 | tf_op jit(solution)/shard_map/all_to_all | solution.py:109
  23.9 5.1 %copy-start.3 = (bf16[8,1,128,2,128]{4,2,3,0,1:T(8,128)(2,1)S(1)}, bf16[8,1,128,2,128]{4,2,3,0,1:T(8,128)(2,1)}, u32[]{:S(2)}) copy-start(bf16[8,1,128,2,128]{4,2,3,0,1:T(8,128)(2,1)} %copy_dynamic-update-slice_fusion) | copy-start | bytes 1572868
  25.2 13.8 %collective-permute-start.7 = (bf16[1,128,2,128]{3,1,2,0:T(8,128)(2,1)S(1)}, bf16[1,128,2,128]{3,1,2,0:T(8,128)(2,1)S(1)}, u32[]{:S(2)}, u32[]{:S(2)}) collective-permute-start(bf16[1,128,2,128]{3,1,2,0:T(8,128)(2,1)S(1)} %bitcast.78), channel_id=1, source_target_pairs={{0,12},{2,14},{4,8},{6,10},{8,4},{10,6},{12,0},{14,2},{1,13},{3,15... | collective-permute-start | bytes 196616 | tf_op jit(solution)/shard_map/ppermute | solution.py:28
  29.8 9.1 %collective-permute-start.8 = (bf16[1,128,2,128]{3,1,2,0:T(8,128)(2,1)S(1)}, bf16[1,128,2,128]{3,1,2,0:T(8,128)(2,1)S(1)}, u32[]{:S(2)}, u32[]{:S(2)}) collective-permute-start(bf16[1,128,2,128]{3,1,2,0:T(8,128)(2,1)S(1)} %bitcast.77), channel_id=1, source_target_pairs={{0,14},{2,12},{4,10},{6,8},{8,6},{10,4},{12,2},{14,0},{1,15},{3,13... | collective-permute-start | bytes 196616 | tf_op jit(solution)/shard_map/ppermute | solution.py:28
  32.2 15.1 %collective-permute-start = (bf16[1024,256]{1,0:T(8,128)(2,1)}, bf16[1024,256]{1,0:T(8,128)(2,1)}, u32[]{:S(2)}, u32[]{:S(2)}) collective-permute-start(bf16[1024,256]{1,0:T(8,128)(2,1)} %get-tuple-element.89), channel_id=1, source_target_pairs={{0,2},{2,4},{4,6},{6,8},{8,10},{10,12},{12,14},{1,3},{3,5},{5,7},{... | collective-permute-start | bytes 1572872 | tf_op jit(solution)/shard_map/ppermute | solution.py:36
  35.8 22.0 %collective-permute-start.1 = (bf16[1024,256]{0,1:T(8,128)(2,1)S(1)}, bf16[1024,256]{0,1:T(8,128)(2,1)}, u32[]{:S(2)}, u32[]{:S(2)}) collective-permute-start(bf16[1024,256]{0,1:T(8,128)(2,1)S(1)} %bitcast.70), channel_id=1, source_target_pairs={{0,2},{2,4},{4,6},{6,8},{8,10},{10,12},{12,14},{1,3},{3,5},{5,7},{... | collective-permute-start | bytes 1572872 | tf_op jit(solution)/shard_map/ppermute | solution.py:36
  49.7 18.9 %all-to-all-start.1 = ((bf16[1,1024,2,128]{3,2,0,1:T(2,128)(2,1)}), bf16[1,1024,2,128]{3,2,0,1:T(2,128)(2,1)S(1)}, u32[]{:S(2)}, u32[]{:S(2)}) async-start(bf16[1,1024,2,128]{3,2,0,1:T(2,128)(2,1)} %copy.99), calls=%async_computation.1 | async-start | bytes 1048576 | tf_op jit(solution)/shard_map/all_to_all | solution.py:110
  69.1 8.2 %copy-start.1 = (bf16[2048,2,128]{0,2,1:T(8,128)(2,1)S(1)}, bf16[2048,2,128]{0,2,1:T(8,128)(2,1)}, u32[]{:S(2)}) copy-start(bf16[2048,2,128]{0,2,1:T(8,128)(2,1)} %pad_maximum_fusion) | copy-start | bytes 3145732
  69.1 8.2 %copy-start.2 = (bf16[2048,2,128]{0,2,1:T(8,128)(2,1)S(1)}, bf16[2048,2,128]{0,2,1:T(8,128)(2,1)}, u32[]{:S(2)}) copy-start(bf16[2048,2,128]{0,2,1:T(8,128)(2,1)} %pad_maximum_fusion.1) | copy-start | bytes 3145732
  70.3 37.0 %all-to-all-start.2 = ((bf16[8,128,2,128]{3,2,1,0:T(2,128)(2,1)}), bf16[8,128,2,128]{3,2,1,0:T(2,128)(2,1)S(1)}, u32[]{:S(2)}, u32[]{:S(2)}) async-start(bf16[8,128,2,128]{3,2,1,0:T(2,128)(2,1)} %copy.103), calls=%async_computation.2 | async-start | bytes 1048576 | tf_op jit(solution)/shard_map/all_to_all | solution.py:112
